TPU v7x, 512 devices: a whole 4x4x16 slice. The times are simulated.
512 devices in a mesh: param: 32 (over y_lo, z), row: 4 (over x), col: 4 (over y_hi, core).
Axes of the slice: x: 4, y: 4 (y_hi: 2, y_lo: 2; y = y_hi * 2 + y_lo), z: 16, core: 2. Of those that a mesh axis runs over, the one named last changes fastest.
Arguments:
- coefficients: bfloat16 [3, 2, 32, 512], P(None, None, 'row', 'col'), may hold values from -6 to 6
- noise_sigma: float32 [2, 32, 512], P(None, 'row', 'col'), may hold values from 0.5 to 4
- residual: float32 [2, 32, 512], P(None, 'row', 'col'), may hold values from -0.6 to 0.6
- crack_mask: int32 [32, 4], P('row', 'col'), may hold values 0 or 1
- node_panel: bfloat16 [4, 64, 3, 2048], P('row', 'col', None, 'param'), may hold values from -0.41992188 to 0.41992188
Outputs:
- hessian: float32 [2048, 2048], P('param', ('row', 'col'))
- gradient: float32 [2048], P(('param', 'row', 'col'))
All inputs are finite; a program needn't handle non-finite values. No bound on the sum of `crack_mask` on one device may be relied on, other than what follows from the above.
Results may differ from a plain program's by a relative error of at most 0.0055.
Values may be sent and summed in bfloat16 or wider, within the bound.
No kernel may reach another device: no remote copies, remote signals or barrier semaphores. Data moves between devices by JAX's collectives and lax.ppermute only.
A program may use at most 64 MiB of HBM per device.

v0:
```python
import jax
import jax.numpy as jnp
from jax import lax
from jax.sharding import PartitionSpec as P

EL = 8
CAMS = 2


def shifted(block, axis, distance):
    devices = range(lax.axis_size(axis))
    route = [(i - distance, i) for i in devices if i - distance in devices]
    return lax.ppermute(block, axis, route)


def corner_shapes(rows, cols):
    vertical = ((jnp.arange(rows) % EL).astype(jnp.float32) + 0.5) / EL
    horizontal = ((jnp.arange(cols) % EL).astype(jnp.float32) + 0.5) / EL
    lower = vertical[:, None]
    right = horizontal[None, :]
    return jnp.stack(
        [(1.0 - lower) * (1.0 - right), (1.0 - lower) * right, lower * (1.0 - right), lower * right]
    )


def pixel_rows(design, extended):
    corners = jnp.stack(
        [extended[:-1, :-1], extended[:-1, 1:], extended[1:, :-1], extended[1:, 1:]], axis=2
    )
    width = extended.shape[3]
    corners = corners.reshape(design.shape[1], 12, width)
    sensitivity = jnp.einsum("kep,ekq->epq", design, corners, preferred_element_type=jnp.float32)
    return sensitivity.astype(jnp.bfloat16).reshape(design.shape[1] * design.shape[2], width)


def block_product(own_rows, other_rows):
    return lax.dot_general(
        own_rows, other_rows, (((0,), (0,)), ((), ())), preferred_element_type=jnp.float32
    )


def on_device(coefficients, noise_sigma, residual, crack_mask, node_panel):
    rows = noise_sigma.shape[1]
    cols = noise_sigma.shape[2]
    elem_rows = rows // EL
    elem_cols = cols // EL
    shapes = corner_shapes(rows, cols)
    live_rows = jnp.repeat(crack_mask.astype(jnp.float32), 128, axis=1)
    pixel_scale = live_rows[None] / noise_sigma
    design = (
        shapes[:, None, None] * pixel_scale[None, None] * coefficients.astype(jnp.float32)[None]
    ).astype(jnp.bfloat16)
    design = design.reshape(4, 3, CAMS, elem_rows, EL, elem_cols, EL).transpose(0, 1, 3, 5, 2, 4, 6)
    design = design.reshape(12, elem_rows * elem_cols, CAMS * EL * EL)
    weighted = (pixel_scale * residual).astype(jnp.bfloat16)
    weighted = (
        weighted.reshape(CAMS, elem_rows, EL, elem_cols, EL).transpose(1, 3, 0, 2, 4).reshape(-1)
    )
    right_edge = shifted(node_panel[:, :1], "col", -1)
    widened = jnp.concatenate([node_panel, right_edge], axis=1)
    lower_edge = shifted(widened, "row", -1)
    extended = jnp.concatenate([widened, lower_edge], axis=0)
    own_rows = pixel_rows(design, extended)
    grad_part = jnp.dot(weighted, own_rows, preferred_element_type=jnp.float32)
    block = block_product(
        own_rows, pixel_rows(design, lax.all_gather(extended, "param", axis=3, tiled=True))
    )
    hessian, gradient = (
        lax.psum_scatter(block, ("row", "col"), scatter_dimension=1, tiled=True),
        lax.psum_scatter(grad_part, ("row", "col"), scatter_dimension=0, tiled=True),
    )
    return (hessian, gradient)


def solution(mesh):
    in_specs = (
        P(None, None, "row", "col"),
        P(None, "row", "col"),
        P(None, "row", "col"),
        P("row", "col"),
        P("row", "col", None, "param"),
    )
    out_specs = (P("param", ("row", "col")), P(("param", "row", "col")))
    return jax.shard_map(
        on_device, mesh=mesh, in_specs=in_specs, out_specs=out_specs, check_vma=False
    )
```

profile of v0, /device:TPU:2, one launch (start us, length us, event | category | flops | bytes accessed | tf_op | source)
XLA Modules:
  0.0 247.3 jit_solution(17997718687711013562)
XLA Ops:
  7.2 0.7 slice.24
  7.9 1.3 collective-permute-start
  9.2 0.7 convert_bitcast_fusion
  9.9 0.8 multiply_convert_fusion.1
  10.9 0.9 reshape.255
  12.2 0.7 constant_dynamic-update-slice_fusion.1
  12.9 0.8 copy.30
  13.8 7.8 %collective-permute-start.1 = (bf16[1,17,3,64]{3,1,2,0:T(8,128)(2,1)S(1)}, bf16[1,17,3,64]{3,1,2,0:T(8,128)(2,1)S(1)}, u32[]{:S(2)}, u32[]{:S(2)}) collective-permute-start(bf16[1,17,3,64]{3,1,2,0:T(8,128)(2,1)S(1)} %constant_dynamic-update-slice_fusion), channel_id=1, source_target_pairs={{4,0},{8,4},{12,8},{5,1},{9,5},{13,9},{6,2},{10,6},{14,10},{7,3},{... | collective-permute-start | bytes 19592 | tf_op jit(solution)/shard_map/ppermute | solution.py:13
  21.5 0.6 slice_bitcast_fusion.2
  22.2 0.8 collective-permute-done.1
  23.8 85.1 %all_gather.3 = bf16[2,17,3,2048]{1,0,2,3:T(2,128)(2,1)S(1)} all-gather(bf16[2,17,3,64]{1,0,2,3:T(2,128)(2,1)S(1)} %copy.32), channel_id=1, replica_groups=mesh['param'=32,'row'=4,'col'=4] {'param'}, dimensions={3}, use_global_device_ids=true | all-gather | bytes 430848 | tf_op jit(solution)/shard_map/all_gather | solution.py:66
  108.9 13.9 %fusion.21 = (bf16[1,16,3,2048]{1,0,2,3:T(2,128)(2,1)}, bf16[1,16,3,2048]{1,0,2,3:T(2,128)(2,1)}, bf16[1,16,3,2048]{1,0,2,3:T(2,128)(2,1)}, bf16[1,16,3,2048]{1,0,2,3:T(2,128)(2,1)S(1)}) fusion(bf16[2,17,3,2048]{1,0,2,3:T(2,128)(2,1)S(1)} %all_gather.3), kind=kLoop, calls=%fused_computation.42 | loop fusion | bytes 1572864 | tf_op jit(solution)/shard_map/slice | solution.py:28
  122.8 6.5 %copy.41 = bf16[1,16,3,2048]{3,1,2,0:T(8,128)(2,1)S(1)} copy(bf16[1,16,3,2048]{1,0,2,3:T(2,128)(2,1)} %get-tuple-element.4) | data formatting | bytes 393216
  129.2 6.5 %copy.43 = bf16[1,16,3,2048]{3,1,2,0:T(8,128)(2,1)S(1)} copy(bf16[1,16,3,2048]{1,0,2,3:T(2,128)(2,1)} %get-tuple-element.5) | data formatting | bytes 393216
  135.7 7.8 %copy.42 = bf16[1,16,3,2048]{3,1,2,0:T(8,128)(2,1)} copy(bf16[1,16,3,2048]{1,0,2,3:T(2,128)(2,1)} %get-tuple-element.6) | data formatting | bytes 393216
  143.5 5.6 %copy.44 = bf16[1,16,3,2048]{3,1,2,0:T(8,128)(2,1)} copy(bf16[1,16,3,2048]{1,0,2,3:T(2,128)(2,1)S(1)} %get-tuple-element.7) | data formatting | bytes 393216
  149.1 0.8 slice_bitcast_fusion.1
  149.9 0.7 pad_maximum_fusion.2
  150.6 1.1 convolution_convert_fusion
  151.7 1.1 pad_maximum_fusion
  152.9 5.4 %fusion.4 = f32[64,2048]{1,0:T(8,128)} fusion(bf16[16,128,64]{1,2,0:T(8,128)(2,1)S(1)} %convolution_convert_fusion, bf16[12,16,128]{2,0,1:T(8,128)(2,1)} %copy.30, bf16[16,12,2048]{2,0,1:T(8,128)(2,1)S(1)} %bitcast.44), kind=kOutput, calls=%fused_computation.3 | convolution fusion | flops 641728512 | bytes 1622016 | tf_op jit(solution)/shard_map/dot_general | solution.py:37
  158.6 1.3 dynamic-slice
  160.7 29.3 %all-reduce = f32[64]{0:T(128)S(1)} all-reduce(f32[64]{0:T(128)S(1)} %convolution_bitcast_fusion), channel_id=3, replica_groups=mesh['param'=32,'row'=4,'col'=4] {'row','col'}, use_global_device_ids=true, to_apply=%region_1.2.clone | all-reduce | flops 64 | bytes 512
  190.6 49.9 %reduce-scatter.2.cloned.1.call-done = f32[64,128]{1,0:T(8,128)} async-done(((f32[64,2048]{1,0:T(8,128)}), f32[64,128]{1,0:T(8,128)}) %reduce-scatter.2.cloned.1.call-update) | async-done | bytes 32784 | tf_op jit(solution)/shard_map/reduce_scatter | solution.py:69
  (24 shorter events, 2.4 us)
Async XLA Ops:
  7.2 233.3 %reduce-scatter.2.cloned.1.call-start = ((), (), s32[]{:S(2)}) async-start(), calls=%async_computation.1 | async-start | bytes 557056 | tf_op jit(solution)/shard_map/reduce_scatter | solution.py:69
  7.9 5.8 %collective-permute-start = (bf16[1,1,3,64]{3,1,2,0:T(2,128)(2,1)S(1)}, bf16[1,1,3,64]{3,1,2,0:T(2,128)(2,1)S(1)}, u32[]{:S(2)}, u32[]{:S(2)}) collective-permute-start(bf16[1,1,3,64]{3,1,2,0:T(2,128)(2,1)S(1)} %slice.24), channel_id=1, source_target_pairs={{1,0},{2,1},{3,2},{5,4},{6,5},{7,6},{9,8},{10,9},{11,10},{13,12},{... | collective-permute-start | bytes 1160 | tf_op jit(solution)/shard_map/ppermute | solution.py:13
  13.8 9.2 %collective-permute-start.1 = (bf16[1,17,3,64]{3,1,2,0:T(8,128)(2,1)S(1)}, bf16[1,17,3,64]{3,1,2,0:T(8,128)(2,1)S(1)}, u32[]{:S(2)}, u32[]{:S(2)}) collective-permute-start(bf16[1,17,3,64]{3,1,2,0:T(8,128)(2,1)S(1)} %constant_dynamic-update-slice_fusion), channel_id=1, source_target_pairs={{4,0},{8,4},{12,8},{5,1},{9,5},{13,9},{6,2},{10,6},{14,10},{7,3},{... | collective-permute-start | bytes 19592 | tf_op jit(solution)/shard_map/ppermute | solution.py:13
  23.0 0.6 copy-start
  135.7 14.2 %copy-start.1 = (bf16[1,16,3,64]{3,1,2,0:T(8,128)(2,1)S(1)}, bf16[1,16,3,64]{3,1,2,0:T(8,128)(2,1)}, u32[]{:S(2)}) copy-start(bf16[1,16,3,64]{3,1,2,0:T(8,128)(2,1)} %param.9) | copy-start | bytes 18436
Sparse Core Ops, SparseCore 0:
  158.4 81.9 reduce-scatter.1
where the time goes:
time: 248 us; the launch traced here: 247 us
  blocking collectives  114 us (46%)
  waiting for transfers between devices  50.7 us (20%)
  local copies, waits for them, and re-layouts  48 us (19%)
  between operations  14.8 us (6%)
  starting transfers between devices  9.1 us (4%)
  matrix products  6.69 us (3%)
  other arithmetic  3.54 us (1%)
    all_gather x1, blocking collectives, on_device(): lax.all_gather(extended, 'param', axis=3, tiled=True)  85.1 us
    reduce_scatter x1, waiting for transfers between devices, on_device(): lax.psum_scatter(block, ('row', 'col'), scatter_dimension=1, tiled=True)  49.9 us
    unnamed x11, local copies, waits for them, and re-layouts  29.5 us
    unnamed x1, blocking collectives  29.3 us
    slice x1, local copies, waits for them, and re-layouts, pixel_rows(): extended[:-1, :-1]  13.9 us
    ppermute x2, starting transfers between devices, shifted(): return lax.ppermute(block, axis, route)  9.07 us
    dot_general x1, matrix products, block_product(): lax.dot_general(own_rows, other_rows, (((0,), (0,)), ((), ())), preferred...  5.42 us
  transfers between devices with their start and end apart: 3, of which 2 were waited for; matrix products, arithmetic and copies ran while one was open for 3% of the time, Pallas kernels for 0%

commit v1 on v0

--- a/solution.py
+++ b/solution.py
@@ -62,9 +62,19 @@
     extended = jnp.concatenate([widened, lower_edge], axis=0)
     own_rows = pixel_rows(design, extended)
     grad_part = jnp.dot(weighted, own_rows, preferred_element_type=jnp.float32)
-    block = block_product(
-        own_rows, pixel_rows(design, lax.all_gather(extended, "param", axis=3, tiled=True))
-    )
+
+    def manage_domain(x_local):
+        return jnp.concatenate(
+            lax.all_to_all(
+                jnp.stack([x_local for _ in range(lax.axis_size("param"))], axis=0),
+                axis_name="param",
+                split_axis=0,
+                concat_axis=0,
+            ),
+            axis=3,
+        )
+
+    block = block_product(own_rows, pixel_rows(design, manage_domain(extended)))
     hessian, gradient = (
         lax.psum_scatter(block, ("row", "col"), scatter_dimension=1, tiled=True),
         lax.psum_scatter(grad_part, ("row", "col"), scatter_dimension=0, tiled=True),

time: 248 us -> 161 us (0.65)
  blocking collectives: 114 us -> 28.6 us
  local copies, waits for them, and re-layouts: 48 us -> 10.8 us
  waiting for transfers between devices: 50.7 us -> 77.2 us
  starting transfers between devices: 9.1 us -> 22 us
    all_gather x1 -> x0, blocking collectives: 85.1 us -> none  [on_device(): lax.all_gather(extended, 'param', axis=3, tiled=True)]
    all_to_all x0 -> x1, waiting for transfers between devices: none -> 26.9 us  [manage_domain(): lax.all_to_all(jnp.stack([x_local for _ in range(lax.axis_size('param'))]...]
    unnamed x11 -> x8, local copies, waits for them, and re-layouts: 29.5 us -> 5.44 us
    slice x1, local copies, waits for them, and re-layouts: 13.9 us -> 0.97 us  [pixel_rows(): extended[:-1, :-1]]
    all_to_all x0 -> x1, starting transfers between devices: none -> 12.9 us  [manage_domain(): lax.all_to_all(jnp.stack([x_local for _ in range(lax.axis_size('param'))]...]
  transfers between devices with their start and end apart: 3 -> 4, of which waited for: 2 -> 3; matrix products, arithmetic and copies ran while one was open for 3% -> 4% of each run, Pallas kernels for 0% -> 0%
where the time goes in v1:
time: 161 us; the launch traced here: 160 us
  waiting for transfers between devices  77.2 us (48%)
  blocking collectives  28.6 us (18%)
  starting transfers between devices  22 us (14%)
  between operations  14.9 us (9%)
  local copies, waits for them, and re-layouts  10.8 us (7%)
  matrix products  5.02 us (3%)
  other arithmetic  1.79 us (1%)
    reduce_scatter x1, waiting for transfers between devices, on_device(): lax.psum_scatter(block, ('row', 'col'), scatter_dimension=1, tiled=True)  50.1 us
    unnamed x1, blocking collectives  28.6 us
    all_to_all x1, waiting for transfers between devices, manage_domain(): lax.all_to_all(jnp.stack([x_local for _ in range(lax.axis_size('param'))]...  26.9 us
    all_to_all x1, starting transfers between devices, manage_domain(): lax.all_to_all(jnp.stack([x_local for _ in range(lax.axis_size('param'))]...  12.9 us
    ppermute x2, starting transfers between devices, shifted(): return lax.ppermute(block, axis, route)  9.07 us
    unnamed x8, local copies, waits for them, and re-layouts  5.44 us
    dot_general x1, matrix products, block_product(): lax.dot_general(own_rows, other_rows, (((0,), (0,)), ((), ())), preferred...  4.58 us
  transfers between devices with their start and end apart: 4, of which 3 were waited for; matrix products, arithmetic and copies ran while one was open for 4% of the time, Pallas kernels for 0%

profile of v1, /device:TPU:2, one launch (start us, length us, event | category | flops | bytes accessed | tf_op | source)
XLA Modules:
  0.0 160.3 jit_solution(477045634303549122)
XLA Ops:
  7.2 0.7 slice.24
  7.9 1.3 collective-permute-start
  9.1 0.7 constant_dynamic-update-slice_fusion.1
  9.9 0.7 convert_bitcast_fusion
  10.5 0.8 multiply_convert_fusion.1
  11.3 7.8 %collective-permute-start.1 = (bf16[1,17,3,64]{3,1,2,0:T(8,128)(2,1)S(1)}, bf16[1,17,3,64]{3,1,2,0:T(8,128)(2,1)S(1)}, u32[]{:S(2)}, u32[]{:S(2)}) collective-permute-start(bf16[1,17,3,64]{3,1,2,0:T(8,128)(2,1)S(1)} %constant_dynamic-update-slice_fusion), channel_id=1, source_target_pairs={{4,0},{8,4},{12,8},{5,1},{9,5},{13,9},{6,2},{10,6},{14,10},{7,3},{... | collective-permute-start | bytes 19592 | tf_op jit(solution)/shard_map/ppermute | solution.py:13
  19.3 0.9 reshape.265
  20.6 0.4 broadcast_bitcast_fusion
  21.1 1.3 reshape.271
  22.4 12.9 %all-to-all-start = ((bf16[32,2,3264]{2,1,0:T(2,128)(2,1)}), bf16[32,2,3264]{2,1,0:T(2,128)(2,1)S(1)}, u32[]{:S(2)}, u32[]{:S(2)}) async-start(bf16[32,2,3264]{2,1,0:T(2,128)(2,1)} %reshape.271), calls=%async_computation | async-start | bytes 851968 | tf_op jit(solution)/shard_map/all_to_all | solution.py:68
  35.9 0.3 copy-done
  36.2 0.3 convolution_convert_fusion
  36.5 26.9 %all-to-all-done = bf16[32,2,3264]{2,1,0:T(2,128)(2,1)S(1)} async-done(((bf16[32,2,3264]{2,1,0:T(2,128)(2,1)}), bf16[32,2,3264]{2,1,0:T(2,128)(2,1)S(1)}, u32[]{:S(2)}, u32[]{:S(2)}) %all-to-all-start) | async-done | bytes 417824 | tf_op jit(solution)/shard_map/all_to_all | solution.py:68
  63.4 0.8 reshape.272
  64.2 0.6 bitcast_bitcast_fusion
  65.0 0.6 reshape.260
  65.6 1.0 fusion.21
  66.6 0.2 copy_bitcast_fusion.2
  66.8 0.2 copy_bitcast_fusion
  67.2 4.6 %fusion.4 = f32[64,2048]{1,0:T(8,128)} fusion(bf16[16,128,64]{1,2,0:T(8,128)(2,1)S(1)} %convolution_convert_fusion, bf16[12,16,128]{2,0,1:T(8,128)(2,1)S(1)} %copy.82, bf16[16,12,2048]{2,0,1:T(8,128)(2,1)S(1)} %bitcast.54), kind=kOutput, calls=%fused_computation.3 | convolution fusion | flops 641728512 | bytes 1622016 | tf_op jit(solution)/shard_map/dot_general | solution.py:37
  72.0 1.3 dynamic-slice
  74.1 28.6 %all-reduce = f32[64]{0:T(128)S(1)} all-reduce(f32[64]{0:T(128)S(1)} %convolution_bitcast_fusion), channel_id=3, replica_groups=mesh['param'=32,'row'=4,'col'=4] {'row','col'}, use_global_device_ids=true, to_apply=%region_1.2.clone | all-reduce | flops 64 | bytes 512
  102.8 0.6 dynamic-slice.1
  103.3 50.1 %reduce-scatter.2.cloned.1.call-done = f32[64,128]{1,0:T(8,128)} async-done(((f32[64,2048]{1,0:T(8,128)}), f32[64,128]{1,0:T(8,128)}) %reduce-scatter.2.cloned.1.call-update) | async-done | bytes 32784 | tf_op jit(solution)/shard_map/reduce_scatter | solution.py:79
  (27 shorter events, 1.8 us)
Async XLA Ops:
  7.9 3.5 %collective-permute-start = (bf16[1,1,3,64]{3,1,2,0:T(2,128)(2,1)S(1)}, bf16[1,1,3,64]{3,1,2,0:T(2,128)(2,1)S(1)}, u32[]{:S(2)}, u32[]{:S(2)}) collective-permute-start(bf16[1,1,3,64]{3,1,2,0:T(2,128)(2,1)S(1)} %slice.24), channel_id=1, source_target_pairs={{1,0},{2,1},{3,2},{5,4},{6,5},{7,6},{9,8},{10,9},{11,10},{13,12},{... | collective-permute-start | bytes 1160 | tf_op jit(solution)/shard_map/ppermute | solution.py:13
  11.3 9.2 %collective-permute-start.1 = (bf16[1,17,3,64]{3,1,2,0:T(8,128)(2,1)S(1)}, bf16[1,17,3,64]{3,1,2,0:T(8,128)(2,1)S(1)}, u32[]{:S(2)}, u32[]{:S(2)}) collective-permute-start(bf16[1,17,3,64]{3,1,2,0:T(8,128)(2,1)S(1)} %constant_dynamic-update-slice_fusion), channel_id=1, source_target_pairs={{4,0},{8,4},{12,8},{5,1},{9,5},{13,9},{6,2},{10,6},{14,10},{7,3},{... | collective-permute-start | bytes 19592 | tf_op jit(solution)/shard_map/ppermute | solution.py:13
  22.4 41.0 %all-to-all-start = ((bf16[32,2,3264]{2,1,0:T(2,128)(2,1)}), bf16[32,2,3264]{2,1,0:T(2,128)(2,1)S(1)}, u32[]{:S(2)}, u32[]{:S(2)}) async-start(bf16[32,2,3264]{2,1,0:T(2,128)(2,1)} %reshape.271), calls=%async_computation | async-start | bytes 851968 | tf_op jit(solution)/shard_map/all_to_all | solution.py:68
  35.3 118.2 %reduce-scatter.2.cloned.1.call-start = ((), (), s32[]{:S(2)}) async-start(), calls=%async_computation.2 | async-start | bytes 557056 | tf_op jit(solution)/shard_map/reduce_scatter | solution.py:79
  35.5 0.7 copy-start
Sparse Core Ops, SparseCore 0:
  71.9 81.5 reduce-scatter.1
